TPU v7x, 32 devices: a whole 2x2x4 slice. The times are simulated.
32 devices in a mesh: dp: 8 (over z, y), seq: 4 (over x, core).
Axes of the slice: x: 2, y: 2, z: 4, core: 2. Of those that a mesh axis runs over, the one named last changes fastest.
Arguments:
- frames: bfloat16 [8, 512, 1536], P('dp', 'seq'), may hold values from -6 to 6
- lengths: int32 [8, 4], P('dp'), may hold values from 1 to 256, 512 in all within a row
- ln1_gain: float32 [1536], replicated, may hold values from 0.5 to 12
- ln2_gain: float32 [1536], replicated, may hold values from 0.5 to 1.5
- w_qkv: bfloat16 [1536, 3, 1536], P('dp', None, 'seq'), may hold values from -0.15625 to 0.15625
- w_out: bfloat16 [1536, 1536], P('seq', 'dp'), may hold values from -0.15625 to 0.15625
- w_glu: bfloat16 [1536, 2, 1536], P('dp', None, 'seq'), may hold values from -0.15625 to 0.15625
- dw_kernel: bfloat16 [31, 1536], P(None, 'seq'), may hold values from -1 to 1
- w_proj: bfloat16 [1536, 1536], P('seq', 'dp'), may hold values from -0.15625 to 0.15625
Outputs:
- block_out: bfloat16 [8, 512, 1536], P('dp', 'seq')
Inputs may be any that keep to these rules, and one draw needn't show every extreme that they name: `lengths`: each row sums to 512, and its largest entry is 256.
All inputs are finite; a program needn't handle non-finite values.
Results may differ from a plain program's by a relative error of at most 0.013.
The roundings to bfloat16 on the way count: a program that leaves them out, or rounds other values in their place, can miss the bound.
Values may be sent and summed in bfloat16 or wider, within the bound.
No kernel may reach another device: no remote copies, remote signals or barrier semaphores. Data moves between devices by JAX's collectives and lax.ppermute only.
A program may use at most 64 MiB of HBM per device.

v0:
```python
import jax
import jax.numpy as jnp
from jax import lax
from jax.sharding import PartitionSpec as P

HD = 96


def layer_norm(values, gain_vec):
    mean_value = jnp.mean(values, axis=-1, keepdims=True)
    centered = values - mean_value
    variance = jnp.mean(centered * centered, axis=-1, keepdims=True)
    return (centered * lax.rsqrt(variance + 1e-05) * gain_vec).astype(jnp.bfloat16)


def segment_of(record_ends, positions):
    return jnp.sum((positions[:, None] >= record_ends[None, :]).astype(jnp.int32), axis=1)


def seq_gather(block):
    count = lax.axis_size("seq")
    me = lax.axis_index("seq")
    parts = [block]
    for shift in range(1, count):
        parts.append(lax.ppermute(block, "seq", [(i, (i - shift) % count) for i in range(count)]))
    ring = jnp.concatenate(parts + parts, axis=0)
    rows = block.shape[0]
    return lax.dynamic_slice_in_dim(ring, (count - me) % count * rows, count * rows, axis=0)


def seq_scatter_sum(full):
    count = lax.axis_size("seq")
    me = lax.axis_index("seq")
    rows = full.shape[0] // count
    total = lax.dynamic_slice_in_dim(full, me * rows, rows, axis=0).astype(jnp.float32)
    for shift in range(1, count):
        piece = lax.dynamic_slice_in_dim(full, (me + shift) % count * rows, rows, axis=0)
        got = lax.ppermute(piece, "seq", [(i, (i + shift) % count) for i in range(count)])
        total = total + got.astype(jnp.float32)
    return total


def attend(projected, seg_all, head_size):
    group_rows = projected.shape[0]
    block_rows = 512
    heads_here = projected.shape[2] // head_size
    split = projected.reshape(group_rows, 3, heads_here, head_size)
    queries = split[:, 0]
    keys = split[:, 1]
    values = split[:, 2]
    blocks = group_rows // block_rows
    scale = 1.0 / head_size**0.5

    def one_block(block_data):
        query_block, seg_block = block_data
        scores = (
            jnp.einsum("qhe,khe->hqk", query_block, keys, preferred_element_type=jnp.float32)
            * scale
        )
        allowed = seg_block[:, None] == seg_all[None, :]
        scores = jnp.where(allowed[None], scores, -1e30)
        top_score = jnp.max(scores, axis=-1, keepdims=True)
        weights = jnp.exp(scores - top_score)
        probs = (weights / jnp.sum(weights, axis=-1, keepdims=True)).astype(jnp.bfloat16)
        mixed = jnp.einsum("hqk,khe->qhe", probs, values, preferred_element_type=jnp.float32)
        return mixed.astype(jnp.bfloat16).reshape(block_rows, heads_here * head_size)

    result = lax.map(
        one_block,
        (
            queries.reshape(blocks, block_rows, heads_here, head_size),
            seg_all.reshape(blocks, block_rows),
        ),
    )
    return result.reshape(group_rows, heads_here * head_size)


def depthwise(padded, kernel, seg_here, seg_near, count):
    total_acc = jnp.zeros((count, padded.shape[1]), jnp.float32)
    for tap_index in range(kernel.shape[0]):
        window = padded[tap_index : tap_index + count].astype(jnp.float32)
        same = (seg_near[tap_index : tap_index + count] == seg_here)[:, None]
        total_acc = total_acc + jnp.where(same, window * kernel[tap_index].astype(jnp.float32), 0.0)
    return jax.nn.silu(total_acc).astype(jnp.bfloat16)


def on_device(frames, lengths, ln1_gain, ln2_gain, w_qkv, w_out, w_glu, dw_kernel, w_proj):
    frame_rows = frames.shape[1]
    model_width = frames.shape[2]
    seq_count = lax.axis_size("seq")
    group_rows = frame_rows * seq_count
    group_width = model_width // seq_count
    kernel_reach = dw_kernel.shape[0] // 2
    qkv_matrix = lax.all_gather(
        w_qkv.reshape(w_qkv.shape[0], 3 * group_width), "dp", axis=0, tiled=True
    )
    out_local = lax.all_gather(w_out, "dp", axis=1, tiled=True)
    glu_matrix = lax.all_gather(
        w_glu.reshape(w_glu.shape[0], 2 * group_width), "dp", axis=0, tiled=True
    )
    proj_local = lax.all_gather(w_proj, "dp", axis=1, tiled=True)
    inputs = frames[0].astype(jnp.float32)
    record_ends = jnp.cumsum(lengths[0])
    seg_all = segment_of(record_ends, jnp.arange(group_rows, dtype=jnp.int32))
    normed1 = layer_norm(inputs, ln1_gain)
    projected = (
        jnp.dot(seq_gather(normed1), qkv_matrix, preferred_element_type=jnp.float32)
        .astype(jnp.bfloat16)
        .reshape(group_rows, 3, group_width)
    )
    attended = attend(projected, seg_all, HD)
    attn_sum = seq_scatter_sum(
        jnp.dot(attended, out_local, preferred_element_type=jnp.float32).astype(jnp.bfloat16)
    )
    middle = (inputs + attn_sum).astype(jnp.bfloat16)
    normed2 = layer_norm(middle.astype(jnp.float32), ln2_gain)
    shard_piece = seq_gather(normed2)
    paired = jnp.dot(shard_piece, glu_matrix, preferred_element_type=jnp.float32).reshape(
        shard_piece.shape[0], 2, group_width
    )
    gated = (paired[:, 0] * jax.nn.sigmoid(paired[:, 1])).astype(jnp.bfloat16)
    padded = jnp.pad(gated, ((kernel_reach, kernel_reach), (0, 0)))
    near_positions = jnp.arange(-kernel_reach, group_rows + kernel_reach, dtype=jnp.int32)
    activated = depthwise(
        padded, dw_kernel, seg_all, segment_of(record_ends, near_positions), group_rows
    )
    conv_out = seq_scatter_sum(
        jnp.dot(activated, proj_local, preferred_element_type=jnp.float32).astype(jnp.bfloat16)
    )
    results = [(middle.astype(jnp.float32) + conv_out).astype(jnp.bfloat16)]
    return jnp.stack(results, axis=0)


def solution(mesh):
    in_specs = (
        P("dp", "seq", None),
        P("dp", None),
        P(),
        P(),
        P("dp", None, "seq"),
        P("seq", "dp"),
        P("dp", None, "seq"),
        P(None, "seq"),
        P("seq", "dp"),
    )
    out_specs = P("dp", "seq", None)
    return jax.shard_map(
        on_device, mesh=mesh, in_specs=in_specs, out_specs=out_specs, check_vma=False
    )
```

profile of v0, /device:TPU:1, one launch (start us, length us, event | category | flops | bytes accessed | tf_op | source)
XLA Modules:
  0.0 247.0 jit_solution(16871168828461402253)
XLA Ops:
  6.5 1.9 copy.27
  14.4 2.7 %collective-permute-start.1 = (bf16[128,1536]{1,0:T(8,128)(2,1)S(1)}, bf16[128,1536]{1,0:T(8,128)(2,1)S(1)}, u32[]{:S(2)}, u32[]{:S(2)}) collective-permute-start(bf16[128,1536]{1,0:T(8,128)(2,1)S(1)} %get-tuple-element.62), channel_id=1, source_target_pairs={{0,2},{1,3},{2,0},{3,1},{4,6},{5,7},{6,4},{7,5},{8,10},{9,11},{10,... | collective-permute-start | bytes 1179656 | tf_op jit(solution)/shard_map/ppermute | solution.py:25
  19.0 8.0 %collective-permute-done = bf16[128,1536]{1,0:T(8,128)(2,1)S(1)} collective-permute-done((bf16[128,1536]{1,0:T(8,128)(2,1)S(1)}, bf16[128,1536]{1,0:T(8,128)(2,1)S(1)}, u32[]{:S(2)}, u32[]{:S(2)}) %collective-permute-start) | collective-permute-done | bytes 393248 | tf_op jit(solution)/shard_map/ppermute | solution.py:25
  28.6 5.9 %collective-permute-done.2 = bf16[128,1536]{1,0:T(8,128)(2,1)S(1)} collective-permute-done((bf16[128,1536]{1,0:T(8,128)(2,1)S(1)}, bf16[128,1536]{1,0:T(8,128)(2,1)S(1)}, u32[]{:S(2)}, u32[]{:S(2)}) %collective-permute-start.2) | collective-permute-done | bytes 393248 | tf_op jit(solution)/shard_map/ppermute | solution.py:25
  38.4 37.5 %all-gather.5.cloned.1.call-done = bf16[1536,1152]{1,0:T(8,128)(2,1)} async-done(((bf16[192,1152]{1,0:T(8,128)(2,1)}), bf16[1536,1152]{1,0:T(8,128)(2,1)}) %all-gather.5.cloned.1.call-update) | async-done | bytes 3538960 | tf_op jit(solution)/shard_map/all_gather | solution.py:94
  75.9 4.7 %convolution_convert_fusion = bf16[512,1152]{1,0:T(8,128)(2,1)S(1)} fusion(bf16[1536,1152]{1,0:T(8,128)(2,1)} %all-gather.5.cloned.1.call-done, bf16[1024,1536]{1,0:T(8,128)(2,1)} %constant_dynamic-update-slice_fusion, s32[]{:T(128)S(6)} %select_n.147), kind=kOutput, calls=%fused_computation.5 | convolution fusion | flops 1812529152 | bytes 6291460 | tf_op jit(solution)/shard_map/dot_general | solution.py:107
  81.2 3.6 %fusion.45 = (f32[4,512]{1,0:T(4,128)S(1)}, f32[4,512,512]{1,2,0:T(8,128)}) fusion(pred[512,512]{0,1:T(8,128)(4,1)S(1)} %broadcast_compare_fusion, bf16[512,3,4,96]{0,3,2,1:T(8,128)(2,1)S(1)} %bitcast.65), kind=kOutput, calls=%fused_computation.155 | convolution fusion | flops 205521408 | bytes 5251072 | tf_op jit(solution)/shard_map/while/body/eval_jaxpr/sub | solution.py:63
  84.8 2.8 %fusion.9 = bf16[4,96,512]{2,1,0:T(8,128)(2,1)S(1)} fusion(f32[4,512,512]{1,2,0:T(8,128)} %get-tuple-element.103, f32[4,512]{1,0:T(4,128)S(1)} %get-tuple-element.102, bf16[512,3,4,96]{0,3,2,1:T(8,128)(2,1)S(1)} %bitcast.66), kind=kOutput, calls=%fused_computation.15 | convolution fusion | flops 203620352 | bytes 4988928 | tf_op jit(solution)/shard_map/while/body/eval_jaxpr/hqk,khe->qhe/dot_general | solution.py:65
  87.6 29.8 %all-gather.7.cloned.1.call-done = bf16[384,1536]{0,1:T(8,128)(2,1)} async-done(((bf16[384,192]{0,1:T(8,128)(2,1)}), bf16[384,1536]{0,1:T(8,128)(2,1)}) %all-gather.7.cloned.1.call-update) | async-done | bytes 1179664 | tf_op jit(solution)/shard_map/all_gather | solution.py:97
  117.4 2.3 convolution_convert_fusion.2
  119.8 3.1 %collective-permute-start.3 = (bf16[128,1536]{1,0:T(8,128)(2,1)S(1)}, bf16[128,1536]{1,0:T(8,128)(2,1)S(1)}, u32[]{:S(2)}, u32[]{:S(2)}) collective-permute-start(bf16[128,1536]{1,0:T(8,128)(2,1)S(1)} %get-tuple-element.68), channel_id=1, source_target_pairs={{0,1},{1,2},{2,3},{3,0},{4,5},{5,6},{6,7},{7,4},{8,9},{9,10},{10,1... | collective-permute-start | bytes 1179656 | tf_op jit(solution)/shard_map/ppermute | solution.py:38
  124.7 6.4 %collective-permute-done.3 = bf16[128,1536]{1,0:T(8,128)(2,1)S(1)} collective-permute-done((bf16[128,1536]{1,0:T(8,128)(2,1)S(1)}, bf16[128,1536]{1,0:T(8,128)(2,1)S(1)}, u32[]{:S(2)}, u32[]{:S(2)}) %collective-permute-start.3) | collective-permute-done | bytes 393248 | tf_op jit(solution)/shard_map/ppermute | solution.py:38
  131.2 9.5 %collective-permute-done.4 = bf16[128,1536]{1,0:T(8,128)(2,1)} collective-permute-done((bf16[128,1536]{1,0:T(8,128)(2,1)S(1)}, bf16[128,1536]{1,0:T(8,128)(2,1)}, u32[]{:S(2)}, u32[]{:S(2)}) %collective-permute-start.4) | collective-permute-done | bytes 393248 | tf_op jit(solution)/shard_map/ppermute | solution.py:38
  145.5 2.2 collective-permute-start.8
  147.8 8.0 %collective-permute-done.6 = bf16[128,1536]{1,0:T(8,128)(2,1)S(1)} collective-permute-done((bf16[128,1536]{1,0:T(8,128)(2,1)S(1)}, bf16[128,1536]{1,0:T(8,128)(2,1)S(1)}, u32[]{:S(2)}, u32[]{:S(2)}) %collective-permute-start.6) | collective-permute-done | bytes 393248 | tf_op jit(solution)/shard_map/ppermute | solution.py:25
  157.3 5.1 %collective-permute-done.8 = bf16[128,1536]{1,0:T(8,128)(2,1)S(1)} collective-permute-done((bf16[128,1536]{1,0:T(8,128)(2,1)S(1)}, bf16[128,1536]{1,0:T(8,128)(2,1)S(1)}, u32[]{:S(2)}, u32[]{:S(2)}) %collective-permute-start.8) | collective-permute-done | bytes 393248 | tf_op jit(solution)/shard_map/ppermute | solution.py:25
  166.3 4.2 %all-gather.9.cloned.1.call-done = bf16[1536,768]{1,0:T(8,128)(2,1)} async-done(((bf16[192,768]{1,0:T(8,128)(2,1)}), bf16[1536,768]{1,0:T(8,128)(2,1)}) %all-gather.9.cloned.1.call-update) | async-done | bytes 2359312 | tf_op jit(solution)/shard_map/all_gather | solution.py:98
  170.5 4.7 %fusion.6 = f32[512,768]{1,0:T(8,128)} fusion(bf16[1536,768]{1,0:T(8,128)(2,1)} %all-gather.9.cloned.1.call-done, bf16[1024,1536]{1,0:T(8,128)(2,1)} %constant_dynamic-update-slice_fusion.8, s32[]{:T(128)S(6)} %select_n.147), kind=kOutput, calls=%fused_computation.12 | convolution fusion | flops 1207959552 | bytes 5505028 | tf_op jit(solution)/shard_map/dot_general | solution.py:118
  175.1 2.1 reshape.147
  178.9 33.2 %all-gather.11.cloned.1.call-done = bf16[384,1536]{0,1:T(8,128)(2,1)} async-done(((bf16[384,192]{0,1:T(8,128)(2,1)}), bf16[384,1536]{0,1:T(8,128)(2,1)}) %all-gather.11.cloned.1.call-update) | async-done | bytes 1179664 | tf_op jit(solution)/shard_map/all_gather | solution.py:101
  212.2 7.8 %convolution_convert_fusion.1 = bf16[512,1536]{1,0:T(8,128)(2,1)S(1)} fusion(bf16[384,1536]{0,1:T(8,128)(2,1)} %all-gather.11.cloned.1.call-done, bf16[512,384]{1,0:T(8,128)(2,1)S(1)} %fusion.32, f32[384]{0:T(512)S(1)} %get-tuple-element.55, f32[384]{0:T(512)S(1)} %get-tuple-element.56, f32[384]{0:T(512)S(1)} %get-tuple-element.18, ...), kind=kOutput, calls=%fused_computation.6 | convolution fusion | flops 629932032 | bytes 3209216 | tf_op jit(solution)/shard_map/dot_general | solution.py:128
  221.4 2.2 collective-permute-start.11
  223.8 5.1 %collective-permute-done.10 = bf16[128,1536]{1,0:T(8,128)(2,1)S(1)} collective-permute-done((bf16[128,1536]{1,0:T(8,128)(2,1)S(1)}, bf16[128,1536]{1,0:T(8,128)(2,1)S(1)}, u32[]{:S(2)}, u32[]{:S(2)}) %collective-permute-start.10) | collective-permute-done | bytes 393248 | tf_op jit(solution)/shard_map/ppermute | solution.py:38
  228.9 10.6 %collective-permute-done.11 = bf16[128,1536]{1,0:T(8,128)(2,1)S(1)} collective-permute-done((bf16[128,1536]{1,0:T(8,128)(2,1)S(1)}, bf16[128,1536]{1,0:T(8,128)(2,1)S(1)}, u32[]{:S(2)}, u32[]{:S(2)}) %collective-permute-start.11) | collective-permute-done | bytes 393248 | tf_op jit(solution)/shard_map/ppermute | solution.py:38
  (108 shorter events, 30.2 us)
Async XLA Ops:
  6.5 69.3 %all-gather.5.cloned.1.call-start = ((), (), s32[]{:S(2)}) async-start(), calls=%async_computation | async-start | bytes 3981312 | tf_op jit(solution)/shard_map/all_gather | solution.py:94
  8.4 108.9 %all-gather.7.cloned.1.call-start = ((), (), s32[]{:S(2)}) async-start(), calls=%async_computation.1 | async-start | bytes 1327104 | tf_op jit(solution)/shard_map/all_gather | solution.py:97
  9.2 161.3 %all-gather.9.cloned.1.call-start = ((), (), s32[]{:S(2)}) async-start(), calls=%async_computation.2 | async-start | bytes 2654208 | tf_op jit(solution)/shard_map/all_gather | solution.py:98
  11.0 201.1 %all-gather.11.cloned.1.call-start = ((), (), s32[]{:S(2)}) async-start(), calls=%async_computation.3 | async-start | bytes 1327104 | tf_op jit(solution)/shard_map/all_gather | solution.py:101
  14.4 12.7 %collective-permute-start = (bf16[128,1536]{1,0:T(8,128)(2,1)S(1)}, bf16[128,1536]{1,0:T(8,128)(2,1)S(1)}, u32[]{:S(2)}, u32[]{:S(2)}) collective-permute-start(bf16[128,1536]{1,0:T(8,128)(2,1)S(1)} %get-tuple-element.62), channel_id=1, source_target_pairs={{0,3},{1,0},{2,1},{3,2},{4,7},{5,4},{6,5},{7,6},{8,11},{9,8},{10,9... | collective-permute-start | bytes 1179656 | tf_op jit(solution)/shard_map/ppermute | solution.py:25
  14.4 13.4 %collective-permute-start.1 = (bf16[128,1536]{1,0:T(8,128)(2,1)S(1)}, bf16[128,1536]{1,0:T(8,128)(2,1)S(1)}, u32[]{:S(2)}, u32[]{:S(2)}) collective-permute-start(bf16[128,1536]{1,0:T(8,128)(2,1)S(1)} %get-tuple-element.62), channel_id=1, source_target_pairs={{0,2},{1,3},{2,0},{3,1},{4,6},{5,7},{6,4},{7,5},{8,10},{9,11},{10,... | collective-permute-start | bytes 1179656 | tf_op jit(solution)/shard_map/ppermute | solution.py:25
  17.1 17.4 %collective-permute-start.2 = (bf16[128,1536]{1,0:T(8,128)(2,1)S(1)}, bf16[128,1536]{1,0:T(8,128)(2,1)S(1)}, u32[]{:S(2)}, u32[]{:S(2)}) collective-permute-start(bf16[128,1536]{1,0:T(8,128)(2,1)S(1)} %get-tuple-element.62), channel_id=1, source_target_pairs={{0,1},{1,2},{2,3},{3,0},{4,5},{5,6},{6,7},{7,4},{8,9},{9,10},{10,1... | collective-permute-start | bytes 1179656 | tf_op jit(solution)/shard_map/ppermute | solution.py:25
  119.8 11.4 %collective-permute-start.3 = (bf16[128,1536]{1,0:T(8,128)(2,1)S(1)}, bf16[128,1536]{1,0:T(8,128)(2,1)S(1)}, u32[]{:S(2)}, u32[]{:S(2)}) collective-permute-start(bf16[128,1536]{1,0:T(8,128)(2,1)S(1)} %get-tuple-element.68), channel_id=1, source_target_pairs={{0,1},{1,2},{2,3},{3,0},{4,5},{5,6},{6,7},{7,4},{8,9},{9,10},{10,1... | collective-permute-start | bytes 1179656 | tf_op jit(solution)/shard_map/ppermute | solution.py:38
  122.8 17.9 %collective-permute-start.4 = (bf16[128,1536]{1,0:T(8,128)(2,1)S(1)}, bf16[128,1536]{1,0:T(8,128)(2,1)}, u32[]{:S(2)}, u32[]{:S(2)}) collective-permute-start(bf16[128,1536]{1,0:T(8,128)(2,1)S(1)} %get-tuple-element.70), channel_id=1, source_target_pairs={{0,2},{1,3},{2,0},{3,1},{4,6},{5,7},{6,4},{7,5},{8,10},{9,11},{10,... | collective-permute-start | bytes 1179656 | tf_op jit(solution)/shard_map/ppermute | solution.py:38
  123.1 18.2 %collective-permute-start.5 = (bf16[128,1536]{1,0:T(8,128)(2,1)S(1)}, bf16[128,1536]{1,0:T(8,128)(2,1)}, u32[]{:S(2)}, u32[]{:S(2)}) collective-permute-start(bf16[128,1536]{1,0:T(8,128)(2,1)S(1)} %get-tuple-element.69), channel_id=1, source_target_pairs={{0,3},{1,0},{2,1},{3,2},{4,7},{5,4},{6,5},{7,6},{8,11},{9,8},{10,9... | collective-permute-start | bytes 1179656 | tf_op jit(solution)/shard_map/ppermute | solution.py:38
  144.0 11.7 %collective-permute-start.6 = (bf16[128,1536]{1,0:T(8,128)(2,1)S(1)}, bf16[128,1536]{1,0:T(8,128)(2,1)S(1)}, u32[]{:S(2)}, u32[]{:S(2)}) collective-permute-start(bf16[128,1536]{1,0:T(8,128)(2,1)S(1)} %get-tuple-element.58), channel_id=1, source_target_pairs={{0,3},{1,0},{2,1},{3,2},{4,7},{5,4},{6,5},{7,6},{8,11},{9,8},{10,9... | collective-permute-start | bytes 1179656 | tf_op jit(solution)/shard_map/ppermute | solution.py:25
  144.1 12.4 %collective-permute-start.7 = (bf16[128,1536]{1,0:T(8,128)(2,1)S(1)}, bf16[128,1536]{1,0:T(8,128)(2,1)S(1)}, u32[]{:S(2)}, u32[]{:S(2)}) collective-permute-start(bf16[128,1536]{1,0:T(8,128)(2,1)S(1)} %get-tuple-element.58), channel_id=1, source_target_pairs={{0,2},{1,3},{2,0},{3,1},{4,6},{5,7},{6,4},{7,5},{8,10},{9,11},{10,... | collective-permute-start | bytes 1179656 | tf_op jit(solution)/shard_map/ppermute | solution.py:25
  145.5 16.9 %collective-permute-start.8 = (bf16[128,1536]{1,0:T(8,128)(2,1)S(1)}, bf16[128,1536]{1,0:T(8,128)(2,1)S(1)}, u32[]{:S(2)}, u32[]{:S(2)}) collective-permute-start(bf16[128,1536]{1,0:T(8,128)(2,1)S(1)} %get-tuple-element.58), channel_id=1, source_target_pairs={{0,1},{1,2},{2,3},{3,0},{4,5},{5,6},{6,7},{7,4},{8,9},{9,10},{10,1... | collective-permute-start | bytes 1179656 | tf_op jit(solution)/shard_map/ppermute | solution.py:25
  177.3 34.8 %copy-start.5 = (pred[512]{0:T(512)(128)(4,1)S(1)}, pred[512]{0:T(512)(128)(4,1)}, u32[]{:S(2)}) copy-start(pred[512]{0:T(512)(128)(4,1)} %get-tuple-element.71) | copy-start | bytes 1540
  177.3 34.8 %copy-start.6 = (pred[512]{0:T(512)(128)(4,1)S(1)}, pred[512]{0:T(512)(128)(4,1)}, u32[]{:S(2)}) copy-start(pred[512]{0:T(512)(128)(4,1)} %get-tuple-element.72) | copy-start | bytes 1540
  177.3 34.8 %copy-start.7 = (pred[512]{0:T(512)(128)(4,1)S(1)}, pred[512]{0:T(512)(128)(4,1)}, u32[]{:S(2)}) copy-start(pred[512]{0:T(512)(128)(4,1)} %get-tuple-element.73) | copy-start | bytes 1540
  177.3 34.8 %copy-start.8 = (pred[512]{0:T(512)(128)(4,1)S(1)}, pred[512]{0:T(512)(128)(4,1)}, u32[]{:S(2)}) copy-start(pred[512]{0:T(512)(128)(4,1)} %get-tuple-element.74) | copy-start | bytes 1540
  177.3 34.8 %copy-start.9 = (pred[512]{0:T(512)(128)(4,1)S(1)}, pred[512]{0:T(512)(128)(4,1)}, u32[]{:S(2)}) copy-start(pred[512]{0:T(512)(128)(4,1)} %get-tuple-element.75) | copy-start | bytes 1540
  177.3 34.8 %copy-start.10 = (pred[512]{0:T(512)(128)(4,1)S(1)}, pred[512]{0:T(512)(128)(4,1)}, u32[]{:S(2)}) copy-start(pred[512]{0:T(512)(128)(4,1)} %get-tuple-element.76) | copy-start | bytes 1540
  177.3 34.8 %copy-start.11 = (pred[512]{0:T(512)(128)(4,1)S(1)}, pred[512]{0:T(512)(128)(4,1)}, u32[]{:S(2)}) copy-start(pred[512]{0:T(512)(128)(4,1)} %get-tuple-element.77) | copy-start | bytes 1540
  177.3 34.8 %copy-start.12 = (pred[512]{0:T(512)(128)(4,1)S(1)}, pred[512]{0:T(512)(128)(4,1)}, u32[]{:S(2)}) copy-start(pred[512]{0:T(512)(128)(4,1)} %get-tuple-element.78) | copy-start | bytes 1540
  220.2 8.7 %collective-permute-start.10 = (bf16[128,1536]{1,0:T(8,128)(2,1)S(1)}, bf16[128,1536]{1,0:T(8,128)(2,1)S(1)}, u32[]{:S(2)}, u32[]{:S(2)}) collective-permute-start(bf16[128,1536]{1,0:T(8,128)(2,1)S(1)} %get-tuple-element.65), channel_id=1, source_target_pairs={{0,2},{1,3},{2,0},{3,1},{4,6},{5,7},{6,4},{7,5},{8,10},{9,11},{10,... | collective-permute-start | bytes 1179656 | tf_op jit(solution)/shard_map/ppermute | solution.py:38
  221.4 18.1 %collective-permute-start.11 = (bf16[128,1536]{1,0:T(8,128)(2,1)S(1)}, bf16[128,1536]{1,0:T(8,128)(2,1)S(1)}, u32[]{:S(2)}, u32[]{:S(2)}) collective-permute-start(bf16[128,1536]{1,0:T(8,128)(2,1)S(1)} %get-tuple-element.64), channel_id=1, source_target_pairs={{0,3},{1,0},{2,1},{3,2},{4,7},{5,4},{6,5},{7,6},{8,11},{9,8},{10,9... | collective-permute-start | bytes 1179656 | tf_op jit(solution)/shard_map/ppermute | solution.py:38
  223.6 15.9 %collective-permute-start.9 = (bf16[128,1536]{1,0:T(8,128)(2,1)S(1)}, bf16[128,1536]{1,0:T(8,128)(2,1)S(1)}, u32[]{:S(2)}, u32[]{:S(2)}) collective-permute-start(bf16[128,1536]{1,0:T(8,128)(2,1)S(1)} %get-tuple-element.63), channel_id=1, source_target_pairs={{0,1},{1,2},{2,3},{3,0},{4,5},{5,6},{6,7},{7,4},{8,9},{9,10},{10,1... | collective-permute-start | bytes 1179656 | tf_op jit(solution)/shard_map/ppermute | solution.py:38
  (16 other events, 438.8 us)
Sparse Core Ops, SparseCore 0:
  9.5 66.2 all-gather.4
  78.1 39.2 all-gather.6
  119.5 50.8 all-gather.8
  172.5 39.5 all-gather.10
where the time goes:
time: 247 us
  waiting for transfers between devices  165 us (67%)
  matrix products  25.8 us (10%)
  local copies, waits for them, and re-layouts  18.8 us (8%)
  starting transfers between devices  14.8 us (6%)
  between operations  13.6 us (6%)
  other arithmetic  9.38 us (4%)
    all_gather x1, waiting for transfers between devices, on_device(): lax.all_gather(w_qkv.reshape(w_qkv.shape[0], 3 * group_width), 'dp', axis...  37.5 us
    all_gather x1, waiting for transfers between devices, on_device(): proj_local = lax.all_gather(w_proj, 'dp', axis=1, tiled=True)  33.2 us
    ppermute x6, waiting for transfers between devices, seq_scatter_sum(): lax.ppermute(piece, 'seq', [(i, (i + shift) % count) for i in range(count)])  32.3 us
    all_gather x1, waiting for transfers between devices, on_device(): out_local = lax.all_gather(w_out, 'dp', axis=1, tiled=True)  29.8 us
    ppermute x6, waiting for transfers between devices, seq_gather(): lax.ppermute(block, 'seq', [(i, (i - shift) % count) for i in range(count)])  26.9 us
    unnamed x61, local copies, waits for them, and re-layouts  11.2 us
    dot_general x1, matrix products, on_device(): jnp.dot(activated, proj_local, preferred_element_type=jnp.float32)  7.81 us
    ppermute x6, starting transfers between devices, seq_gather(): lax.ppermute(block, 'seq', [(i, (i - shift) % count) for i in range(count)])  7.57 us
  transfers between devices with their start and end apart: 16, of which 13 were waited for; matrix products, arithmetic and copies ran while one was open for 17% of the time, Pallas kernels for 0%

commit v1 on v0

--- a/solution.py
+++ b/solution.py
@@ -94,7 +94,12 @@
     qkv_matrix = lax.all_gather(
         w_qkv.reshape(w_qkv.shape[0], 3 * group_width), "dp", axis=0, tiled=True
     )
-    out_local = lax.all_gather(w_out, "dp", axis=1, tiled=True)
+    ring_ = [w_out]
+    for hop in range(7):
+        ring_.append(lax.ppermute(ring_[-1], "dp", [(dev, (dev + 1) % 8) for dev in range(8)]))
+    out_local = jnp.roll(
+        jnp.concatenate(ring_[::-1], axis=1), (lax.axis_index("dp") + 1) * ring_[0].shape[1], axis=1
+    )
     glu_matrix = lax.all_gather(
         w_glu.reshape(w_glu.shape[0], 2 * group_width), "dp", axis=0, tiled=True
     )

time: 247 us -> 222 us (0.90)
  waiting for transfers between devices: 165 us -> 122 us
  local copies, waits for them, and re-layouts: 18.8 us -> 28.4 us
  starting transfers between devices: 14.8 us -> 22 us
    ppermute x0 -> x7, waiting for transfers between devices: none -> 55.3 us  [on_device(): lax.ppermute(ring_[-1], 'dp', [(dev, (dev + 1) % 8) for dev in range(8)])]
    all_gather x1, waiting for transfers between devices: 37.5 us -> 0.52 us  [on_device(): lax.all_gather(w_qkv.reshape(w_qkv.shape[0], 3 * group_width), 'dp', axis...]
    all_gather x1 -> x0, waiting for transfers between devices: 29.8 us -> none  [on_device(): out_local = lax.all_gather(w_out, 'dp', axis=1, tiled=True)]
    ppermute x6, waiting for transfers between devices: 26.9 us -> 10.2 us  [seq_gather(): lax.ppermute(block, 'seq', [(i, (i - shift) % count) for i in range(count)])]
    all_gather x1, waiting for transfers between devices: 33.2 us -> 21 us  [on_device(): proj_local = lax.all_gather(w_proj, 'dp', axis=1, tiled=True)]
    unnamed x61 -> x118, local copies, waits for them, and re-layouts: 11.2 us -> 21.4 us
    ppermute x6, starting transfers between devices: 7.15 us -> 12.8 us  [seq_scatter_sum(): lax.ppermute(piece, 'seq', [(i, (i + shift) % count) for i in range(count)])]
    all_gather x1, waiting for transfers between devices: 4.18 us -> 0.01 us  [on_device(): lax.all_gather(w_glu.reshape(w_glu.shape[0], 2 * group_width), 'dp', axis...]
  transfers between devices with their start and end apart: 16 -> 22, of which waited for: 13 -> 17; matrix products, arithmetic and copies ran while one was open for 17% -> 24% of each run, Pallas kernels for 0% -> 0%
where the time goes in v1:
time: 222 us
  waiting for transfers between devices  122 us (55%)
  local copies, waits for them, and re-layouts  28.4 us (13%)
  matrix products  25.1 us (11%)
  starting transfers between devices  22 us (10%)
  between operations  14 us (6%)
  other arithmetic  10.8 us (5%)
    ppermute x7, waiting for transfers between devices, on_device(): lax.ppermute(ring_[-1], 'dp', [(dev, (dev + 1) % 8) for dev in range(8)])  55.3 us
    ppermute x6, waiting for transfers between devices, seq_scatter_sum(): lax.ppermute(piece, 'seq', [(i, (i + shift) % count) for i in range(count)])  34.6 us
    unnamed x118, local copies, waits for them, and re-layouts  21.4 us
    all_gather x1, waiting for transfers between devices, on_device(): proj_local = lax.all_gather(w_proj, 'dp', axis=1, tiled=True)  21 us
    ppermute x6, starting transfers between devices, seq_scatter_sum(): lax.ppermute(piece, 'seq', [(i, (i + shift) % count) for i in range(count)])  12.8 us
    ppermute x6, waiting for transfers between devices, seq_gather(): lax.ppermute(block, 'seq', [(i, (i - shift) % count) for i in range(count)])  10.2 us
    dot_general x1, matrix products, on_device(): jnp.dot(activated, proj_local, preferred_element_type=jnp.float32)  8.08 us
    ppermute x6, starting transfers between devices, seq_gather(): lax.ppermute(block, 'seq', [(i, (i - shift) % count) for i in range(count)])  6.36 us
  transfers between devices with their start and end apart: 22, of which 17 were waited for; matrix products, arithmetic and copies ran while one was open for 24% of the time, Pallas kernels for 0%

profile of v1, /device:TPU:1, one launch (start us, length us, event | category | flops | bytes accessed | tf_op | source)
XLA Modules:
  0.0 221.9 jit_solution(12835087239390443769)
XLA Ops:
  11.8 2.7 %collective-permute-start.3 = (bf16[384,192]{0,1:T(8,128)(2,1)S(1)}, bf16[384,192]{0,1:T(8,128)(2,1)S(1)}, u32[]{:S(2)}, u32[]{:S(2)}) collective-permute-start(bf16[384,192]{0,1:T(8,128)(2,1)S(1)} %copy-done.1), channel_id=1, source_target_pairs={{0,4},{4,8},{8,12},{12,16},{16,20},{20,24},{24,28},{28,0},{1,5},{5... | collective-permute-start | bytes 442376 | tf_op jit(solution)/shard_map/ppermute | solution.py:99
  17.7 2.9 %collective-permute-done.3 = bf16[384,192]{0,1:T(8,128)(2,1)S(1)} collective-permute-done((bf16[384,192]{0,1:T(8,128)(2,1)S(1)}, bf16[384,192]{0,1:T(8,128)(2,1)S(1)}, u32[]{:S(2)}, u32[]{:S(2)}) %collective-permute-start.3) | collective-permute-done | bytes 147488 | tf_op jit(solution)/shard_map/ppermute | solution.py:99
  20.8 10.5 %collective-permute-done.4 = bf16[384,192]{0,1:T(8,128)(2,1)S(1)} collective-permute-done((bf16[384,192]{0,1:T(8,128)(2,1)S(1)}, bf16[384,192]{0,1:T(8,128)(2,1)S(1)}, u32[]{:S(2)}, u32[]{:S(2)}) %collective-permute-start.4) | collective-permute-done | bytes 147488 | tf_op jit(solution)/shard_map/ppermute | solution.py:99
  33.7 8.3 %collective-permute-done.5 = bf16[384,192]{0,1:T(8,128)(2,1)S(1)} collective-permute-done((bf16[384,192]{0,1:T(8,128)(2,1)S(1)}, bf16[384,192]{0,1:T(8,128)(2,1)S(1)}, u32[]{:S(2)}, u32[]{:S(2)}) %collective-permute-start.5) | collective-permute-done | bytes 147488 | tf_op jit(solution)/shard_map/ppermute | solution.py:99
  42.7 5.9 %collective-permute-done.6 = bf16[384,192]{0,1:T(8,128)(2,1)S(1)} collective-permute-done((bf16[384,192]{0,1:T(8,128)(2,1)S(1)}, bf16[384,192]{0,1:T(8,128)(2,1)S(1)}, u32[]{:S(2)}, u32[]{:S(2)}) %collective-permute-start.6) | collective-permute-done | bytes 147488 | tf_op jit(solution)/shard_map/ppermute | solution.py:99
  49.4 9.0 %collective-permute-done.7 = bf16[384,192]{0,1:T(8,128)(2,1)S(1)} collective-permute-done((bf16[384,192]{0,1:T(8,128)(2,1)S(1)}, bf16[384,192]{0,1:T(8,128)(2,1)S(1)}, u32[]{:S(2)}, u32[]{:S(2)}) %collective-permute-start.7) | collective-permute-done | bytes 147488 | tf_op jit(solution)/shard_map/ppermute | solution.py:99
  59.3 9.1 %collective-permute-done.8 = bf16[384,192]{0,1:T(8,128)(2,1)S(1)} collective-permute-done((bf16[384,192]{0,1:T(8,128)(2,1)S(1)}, bf16[384,192]{0,1:T(8,128)(2,1)S(1)}, u32[]{:S(2)}, u32[]{:S(2)}) %collective-permute-start.8) | collective-permute-done | bytes 147488 | tf_op jit(solution)/shard_map/ppermute | solution.py:99
  69.2 9.5 %collective-permute-done.9 = bf16[384,192]{0,1:T(8,128)(2,1)S(1)} collective-permute-done((bf16[384,192]{0,1:T(8,128)(2,1)S(1)}, bf16[384,192]{0,1:T(8,128)(2,1)S(1)}, u32[]{:S(2)}, u32[]{:S(2)}) %collective-permute-start.9) | collective-permute-done | bytes 147488 | tf_op jit(solution)/shard_map/ppermute | solution.py:99
  90.0 4.7 %convolution_convert_fusion = bf16[512,1152]{1,0:T(8,128)(2,1)S(1)} fusion(bf16[1536,1152]{1,0:T(8,128)(2,1)} %all-gather.4.cloned.1.call-done, bf16[1024,1536]{1,0:T(8,128)(2,1)} %constant_dynamic-update-slice_fusion, s32[]{:T(128)S(6)} %select_n.159), kind=kOutput, calls=%fused_computation.5 | convolution fusion | flops 1812529152 | bytes 6291460 | tf_op jit(solution)/shard_map/dot_general | solution.py:112
  95.3 3.6 %fusion.47 = (f32[4,512]{1,0:T(4,128)S(1)}, f32[4,512,512]{1,2,0:T(8,128)}) fusion(pred[512,512]{0,1:T(8,128)(4,1)S(1)} %broadcast_compare_fusion, bf16[512,3,4,96]{0,3,2,1:T(8,128)(2,1)S(1)} %bitcast.64), kind=kOutput, calls=%fused_computation.173 | convolution fusion | flops 205521408 | bytes 5251072 | tf_op jit(solution)/shard_map/while/body/eval_jaxpr/sub | solution.py:63
  99.0 2.8 %fusion.9 = bf16[4,96,512]{2,1,0:T(8,128)(2,1)S(1)} fusion(f32[4,512,512]{1,2,0:T(8,128)} %get-tuple-element.103, f32[4,512]{1,0:T(4,128)S(1)} %get-tuple-element.102, bf16[512,3,4,96]{0,3,2,1:T(8,128)(2,1)S(1)} %bitcast.65), kind=kOutput, calls=%fused_computation.15 | convolution fusion | flops 203620352 | bytes 4988928 | tf_op jit(solution)/shard_map/while/body/eval_jaxpr/hqk,khe->qhe/dot_general | solution.py:65
  101.8 2.3 %convolution_convert_fusion.2 = bf16[512,1536]{1,0:T(8,128)(2,1)S(1)} fusion(bf16[512,384]{0,1:T(8,128)(2,1)S(1)} %bitcast.72, bf16[384,3072]{0,1:T(8,128)(2,1)} %constant_dynamic-update-slice_fusion.8, s32[]{:T(128)S(6)} %select_n.162), kind=kOutput, calls=%fused_computation.7 | convolution fusion | flops 604766208 | bytes 3145732 | tf_op jit(solution)/shard_map/dot_general | solution.py:118
  104.2 8.8 %collective-permute-start.10 = (bf16[128,1536]{1,0:T(8,128)(2,1)S(1)}, bf16[128,1536]{1,0:T(8,128)(2,1)}, u32[]{:S(2)}, u32[]{:S(2)}) collective-permute-start(bf16[128,1536]{1,0:T(8,128)(2,1)S(1)} %get-tuple-element.68), channel_id=1, source_target_pairs={{0,1},{1,2},{2,3},{3,0},{4,5},{5,6},{6,7},{7,4},{8,9},{9,10},{10,1... | collective-permute-start | bytes 1179656 | tf_op jit(solution)/shard_map/ppermute | solution.py:38
  114.3 7.0 %collective-permute-done.10 = bf16[128,1536]{1,0:T(8,128)(2,1)} collective-permute-done((bf16[128,1536]{1,0:T(8,128)(2,1)S(1)}, bf16[128,1536]{1,0:T(8,128)(2,1)}, u32[]{:S(2)}, u32[]{:S(2)}) %collective-permute-start.10) | collective-permute-done | bytes 393248 | tf_op jit(solution)/shard_map/ppermute | solution.py:38
  121.4 9.4 %collective-permute-done.11 = bf16[128,1536]{1,0:T(8,128)(2,1)} collective-permute-done((bf16[128,1536]{1,0:T(8,128)(2,1)S(1)}, bf16[128,1536]{1,0:T(8,128)(2,1)}, u32[]{:S(2)}, u32[]{:S(2)}) %collective-permute-start.11) | collective-permute-done | bytes 393248 | tf_op jit(solution)/shard_map/ppermute | solution.py:38
  139.7 2.0 collective-permute-start.15
  141.7 3.7 %collective-permute-done.13 = bf16[128,1536]{1,0:T(8,128)(2,1)S(1)} collective-permute-done((bf16[128,1536]{1,0:T(8,128)(2,1)S(1)}, bf16[128,1536]{1,0:T(8,128)(2,1)S(1)}, u32[]{:S(2)}, u32[]{:S(2)}) %collective-permute-start.13) | collective-permute-done | bytes 393248 | tf_op jit(solution)/shard_map/ppermute | solution.py:25
  146.9 6.5 %collective-permute-done.15 = bf16[128,1536]{1,0:T(8,128)(2,1)S(1)} collective-permute-done((bf16[128,1536]{1,0:T(8,128)(2,1)S(1)}, bf16[128,1536]{1,0:T(8,128)(2,1)S(1)}, u32[]{:S(2)}, u32[]{:S(2)}) %collective-permute-start.15) | collective-permute-done | bytes 393248 | tf_op jit(solution)/shard_map/ppermute | solution.py:25
  157.4 3.5 %fusion.6 = f32[512,768]{1,0:T(8,128)S(1)} fusion(bf16[1536,768]{1,0:T(8,128)(2,1)} %all-gather.6.cloned.1.call-done, bf16[1024,1536]{1,0:T(8,128)(2,1)} %constant_dynamic-update-slice_fusion.24, s32[]{:T(128)S(6)} %select_n.159), kind=kOutput, calls=%fused_computation.12 | convolution fusion | flops 1207959552 | bytes 5505028 | tf_op jit(solution)/shard_map/dot_general | solution.py:123
  163.6 21.0 %all-gather.8.cloned.1.call-done = bf16[384,1536]{0,1:T(8,128)(2,1)} async-done(((bf16[384,192]{0,1:T(8,128)(2,1)}), bf16[384,1536]{0,1:T(8,128)(2,1)}) %all-gather.8.cloned.1.call-update) | async-done | bytes 1179664 | tf_op jit(solution)/shard_map/all_gather | solution.py:106
  185.1 8.1 %convolution_convert_fusion.1 = bf16[512,1536]{1,0:T(8,128)(2,1)S(1)} fusion(bf16[384,1536]{0,1:T(8,128)(2,1)} %all-gather.8.cloned.1.call-done, bf16[512,384]{1,0:T(8,128)(2,1)S(1)} %fusion.33, f32[384]{0:T(512)S(1)} %copy-done.29, f32[384]{0:T(512)S(1)} %copy-done.30, f32[384]{0:T(512)S(1)} %get-tuple-element.18, f32[384]{0:T(512)S(1)} %get-tuple-element.19, ...), kind=kOutput, calls=%fused_computation.6 | convolution fusion | flops 629932032 | bytes 3209216 | tf_op jit(solution)/shard_map/dot_general | solution.py:133
  193.2 3.1 %collective-permute-start.16 = (bf16[128,1536]{1,0:T(8,128)(2,1)S(1)}, bf16[128,1536]{1,0:T(8,128)(2,1)S(1)}, u32[]{:S(2)}, u32[]{:S(2)}) collective-permute-start(bf16[128,1536]{1,0:T(8,128)(2,1)S(1)} %get-tuple-element.63), channel_id=1, source_target_pairs={{0,1},{1,2},{2,3},{3,0},{4,5},{5,6},{6,7},{7,4},{8,9},{9,10},{10,1... | collective-permute-start | bytes 1179656 | tf_op jit(solution)/shard_map/ppermute | solution.py:38
  196.8 7.9 %collective-permute-done.16 = bf16[128,1536]{1,0:T(8,128)(2,1)S(1)} collective-permute-done((bf16[128,1536]{1,0:T(8,128)(2,1)S(1)}, bf16[128,1536]{1,0:T(8,128)(2,1)S(1)}, u32[]{:S(2)}, u32[]{:S(2)}) %collective-permute-start.16) | collective-permute-done | bytes 393248 | tf_op jit(solution)/shard_map/ppermute | solution.py:38
  204.6 9.1 %collective-permute-done.17 = bf16[128,1536]{1,0:T(8,128)(2,1)S(1)} collective-permute-done((bf16[128,1536]{1,0:T(8,128)(2,1)S(1)}, bf16[128,1536]{1,0:T(8,128)(2,1)S(1)}, u32[]{:S(2)}, u32[]{:S(2)}) %collective-permute-start.17) | collective-permute-done | bytes 393248 | tf_op jit(solution)/shard_map/ppermute | solution.py:38
  (177 shorter events, 46.4 us)
Async XLA Ops:
  6.5 83.5 %all-gather.4.cloned.1.call-start = ((), (), s32[]{:S(2)}) async-start(), calls=%async_computation | async-start | bytes 3981312 | tf_op jit(solution)/shard_map/all_gather | solution.py:94
  8.5 148.9 %all-gather.6.cloned.1.call-start = ((), (), s32[]{:S(2)}) async-start(), calls=%async_computation.1 | async-start | bytes 2654208 | tf_op jit(solution)/shard_map/all_gather | solution.py:103
  10.3 174.4 %all-gather.8.cloned.1.call-start = ((), (), s32[]{:S(2)}) async-start(), calls=%async_computation.2 | async-start | bytes 1327104 | tf_op jit(solution)/shard_map/all_gather | solution.py:106
  11.7 19.6 %collective-permute-start = (bf16[128,1536]{1,0:T(8,128)(2,1)S(1)}, bf16[128,1536]{1,0:T(8,128)(2,1)S(1)}, u32[]{:S(2)}, u32[]{:S(2)}) collective-permute-start(bf16[128,1536]{1,0:T(8,128)(2,1)S(1)} %get-tuple-element.62), channel_id=1, source_target_pairs={{0,3},{1,0},{2,1},{3,2},{4,7},{5,4},{6,5},{7,6},{8,11},{9,8},{10,9... | collective-permute-start | bytes 1179656 | tf_op jit(solution)/shard_map/ppermute | solution.py:25
  11.8 8.8 %collective-permute-start.3 = (bf16[384,192]{0,1:T(8,128)(2,1)S(1)}, bf16[384,192]{0,1:T(8,128)(2,1)S(1)}, u32[]{:S(2)}, u32[]{:S(2)}) collective-permute-start(bf16[384,192]{0,1:T(8,128)(2,1)S(1)} %copy-done.1), channel_id=1, source_target_pairs={{0,4},{4,8},{8,12},{12,16},{16,20},{20,24},{24,28},{28,0},{1,5},{5... | collective-permute-start | bytes 442376 | tf_op jit(solution)/shard_map/ppermute | solution.py:99
  14.5 17.6 %collective-permute-start.1 = (bf16[128,1536]{1,0:T(8,128)(2,1)S(1)}, bf16[128,1536]{1,0:T(8,128)(2,1)S(1)}, u32[]{:S(2)}, u32[]{:S(2)}) collective-permute-start(bf16[128,1536]{1,0:T(8,128)(2,1)S(1)} %get-tuple-element.62), channel_id=1, source_target_pairs={{0,2},{1,3},{2,0},{3,1},{4,6},{5,7},{6,4},{7,5},{8,10},{9,11},{10,... | collective-permute-start | bytes 1179656 | tf_op jit(solution)/shard_map/ppermute | solution.py:25
  15.7 17.2 %collective-permute-start.2 = (bf16[128,1536]{1,0:T(8,128)(2,1)S(1)}, bf16[128,1536]{1,0:T(8,128)(2,1)S(1)}, u32[]{:S(2)}, u32[]{:S(2)}) collective-permute-start(bf16[128,1536]{1,0:T(8,128)(2,1)S(1)} %get-tuple-element.62), channel_id=1, source_target_pairs={{0,1},{1,2},{2,3},{3,0},{4,5},{5,6},{6,7},{7,4},{8,9},{9,10},{10,1... | collective-permute-start | bytes 1179656 | tf_op jit(solution)/shard_map/ppermute | solution.py:25
  20.6 10.7 %collective-permute-start.4 = (bf16[384,192]{0,1:T(8,128)(2,1)S(1)}, bf16[384,192]{0,1:T(8,128)(2,1)S(1)}, u32[]{:S(2)}, u32[]{:S(2)}) collective-permute-start(bf16[384,192]{0,1:T(8,128)(2,1)S(1)} %collective-permute-done.3), channel_id=1, source_target_pairs={{0,4},{4,8},{8,12},{12,16},{16,20},{20,24},{24,28},{28,0},{1,5},{5... | collective-permute-start | bytes 442376 | tf_op jit(solution)/shard_map/ppermute | solution.py:99
  31.3 10.6 %collective-permute-start.5 = (bf16[384,192]{0,1:T(8,128)(2,1)S(1)}, bf16[384,192]{0,1:T(8,128)(2,1)S(1)}, u32[]{:S(2)}, u32[]{:S(2)}) collective-permute-start(bf16[384,192]{0,1:T(8,128)(2,1)S(1)} %collective-permute-done.4), channel_id=1, source_target_pairs={{0,4},{4,8},{8,12},{12,16},{16,20},{20,24},{24,28},{28,0},{1,5},{5... | collective-permute-start | bytes 442376 | tf_op jit(solution)/shard_map/ppermute | solution.py:99
  41.9 6.7 %collective-permute-start.6 = (bf16[384,192]{0,1:T(8,128)(2,1)S(1)}, bf16[384,192]{0,1:T(8,128)(2,1)S(1)}, u32[]{:S(2)}, u32[]{:S(2)}) collective-permute-start(bf16[384,192]{0,1:T(8,128)(2,1)S(1)} %collective-permute-done.5), channel_id=1, source_target_pairs={{0,4},{4,8},{8,12},{12,16},{16,20},{20,24},{24,28},{28,0},{1,5},{5... | collective-permute-start | bytes 442376 | tf_op jit(solution)/shard_map/ppermute | solution.py:99
  48.6 9.8 %collective-permute-start.7 = (bf16[384,192]{0,1:T(8,128)(2,1)S(1)}, bf16[384,192]{0,1:T(8,128)(2,1)S(1)}, u32[]{:S(2)}, u32[]{:S(2)}) collective-permute-start(bf16[384,192]{0,1:T(8,128)(2,1)S(1)} %collective-permute-done.6), channel_id=1, source_target_pairs={{0,4},{4,8},{8,12},{12,16},{16,20},{20,24},{24,28},{28,0},{1,5},{5... | collective-permute-start | bytes 442376 | tf_op jit(solution)/shard_map/ppermute | solution.py:99
  58.5 9.9 %collective-permute-start.8 = (bf16[384,192]{0,1:T(8,128)(2,1)S(1)}, bf16[384,192]{0,1:T(8,128)(2,1)S(1)}, u32[]{:S(2)}, u32[]{:S(2)}) collective-permute-start(bf16[384,192]{0,1:T(8,128)(2,1)S(1)} %collective-permute-done.7), channel_id=1, source_target_pairs={{0,4},{4,8},{8,12},{12,16},{16,20},{20,24},{24,28},{28,0},{1,5},{5... | collective-permute-start | bytes 442376 | tf_op jit(solution)/shard_map/ppermute | solution.py:99
  68.4 10.3 %collective-permute-start.9 = (bf16[384,192]{0,1:T(8,128)(2,1)S(1)}, bf16[384,192]{0,1:T(8,128)(2,1)S(1)}, u32[]{:S(2)}, u32[]{:S(2)}) collective-permute-start(bf16[384,192]{0,1:T(8,128)(2,1)S(1)} %collective-permute-done.8), channel_id=1, source_target_pairs={{0,4},{4,8},{8,12},{12,16},{16,20},{20,24},{24,28},{28,0},{1,5},{5... | collective-permute-start | bytes 442376 | tf_op jit(solution)/shard_map/ppermute | solution.py:99
  104.1 29.1 %copy-start.3 = (f32[1536]{0:T(1024)S(1)}, f32[1536]{0:T(1024)}, u32[]{:S(2)}) copy-start(f32[1536]{0:T(1024)} %param.12) | copy-start | bytes 18436
  104.2 17.1 %collective-permute-start.10 = (bf16[128,1536]{1,0:T(8,128)(2,1)S(1)}, bf16[128,1536]{1,0:T(8,128)(2,1)}, u32[]{:S(2)}, u32[]{:S(2)}) collective-permute-start(bf16[128,1536]{1,0:T(8,128)(2,1)S(1)} %get-tuple-element.68), channel_id=1, source_target_pairs={{0,1},{1,2},{2,3},{3,0},{4,5},{5,6},{6,7},{7,4},{8,9},{9,10},{10,1... | collective-permute-start | bytes 1179656 | tf_op jit(solution)/shard_map/ppermute | solution.py:38
  113.0 17.7 %collective-permute-start.11 = (bf16[128,1536]{1,0:T(8,128)(2,1)S(1)}, bf16[128,1536]{1,0:T(8,128)(2,1)}, u32[]{:S(2)}, u32[]{:S(2)}) collective-permute-start(bf16[128,1536]{1,0:T(8,128)(2,1)S(1)} %get-tuple-element.70), channel_id=1, source_target_pairs={{0,2},{1,3},{2,0},{3,1},{4,6},{5,7},{6,4},{7,5},{8,10},{9,11},{10,... | collective-permute-start | bytes 1179656 | tf_op jit(solution)/shard_map/ppermute | solution.py:38
  113.2 18.2 %collective-permute-start.12 = (bf16[128,1536]{1,0:T(8,128)(2,1)S(1)}, bf16[128,1536]{1,0:T(8,128)(2,1)}, u32[]{:S(2)}, u32[]{:S(2)}) collective-permute-start(bf16[128,1536]{1,0:T(8,128)(2,1)S(1)} %get-tuple-element.69), channel_id=1, source_target_pairs={{0,3},{1,0},{2,1},{3,2},{4,7},{5,4},{6,5},{7,6},{8,11},{9,8},{10,9... | collective-permute-start | bytes 1179656 | tf_op jit(solution)/shard_map/ppermute | solution.py:38
  134.2 11.2 %collective-permute-start.13 = (bf16[128,1536]{1,0:T(8,128)(2,1)S(1)}, bf16[128,1536]{1,0:T(8,128)(2,1)S(1)}, u32[]{:S(2)}, u32[]{:S(2)}) collective-permute-start(bf16[128,1536]{1,0:T(8,128)(2,1)S(1)} %get-tuple-element.58), channel_id=1, source_target_pairs={{0,3},{1,0},{2,1},{3,2},{4,7},{5,4},{6,5},{7,6},{8,11},{9,8},{10,9... | collective-permute-start | bytes 1179656 | tf_op jit(solution)/shard_map/ppermute | solution.py:25
  134.9 11.3 %collective-permute-start.14 = (bf16[128,1536]{1,0:T(8,128)(2,1)S(1)}, bf16[128,1536]{1,0:T(8,128)(2,1)S(1)}, u32[]{:S(2)}, u32[]{:S(2)}) collective-permute-start(bf16[128,1536]{1,0:T(8,128)(2,1)S(1)} %get-tuple-element.58), channel_id=1, source_target_pairs={{0,2},{1,3},{2,0},{3,1},{4,6},{5,7},{6,4},{7,5},{8,10},{9,11},{10,... | collective-permute-start | bytes 1179656 | tf_op jit(solution)/shard_map/ppermute | solution.py:25
  139.7 13.8 %collective-permute-start.15 = (bf16[128,1536]{1,0:T(8,128)(2,1)S(1)}, bf16[128,1536]{1,0:T(8,128)(2,1)S(1)}, u32[]{:S(2)}, u32[]{:S(2)}) collective-permute-start(bf16[128,1536]{1,0:T(8,128)(2,1)S(1)} %get-tuple-element.58), channel_id=1, source_target_pairs={{0,1},{1,2},{2,3},{3,0},{4,5},{5,6},{6,7},{7,4},{8,9},{9,10},{10,1... | collective-permute-start | bytes 1179656 | tf_op jit(solution)/shard_map/ppermute | solution.py:25
  161.8 22.9 %copy-start.4 = (f32[384]{0:T(512)S(1)}, f32[384]{0:T(512)}, u32[]{:S(2)}) copy-start(f32[384]{0:T(512)} %get-tuple-element.28) | copy-start | bytes 4612
  193.2 11.4 %collective-permute-start.16 = (bf16[128,1536]{1,0:T(8,128)(2,1)S(1)}, bf16[128,1536]{1,0:T(8,128)(2,1)S(1)}, u32[]{:S(2)}, u32[]{:S(2)}) collective-permute-start(bf16[128,1536]{1,0:T(8,128)(2,1)S(1)} %get-tuple-element.63), channel_id=1, source_target_pairs={{0,1},{1,2},{2,3},{3,0},{4,5},{5,6},{6,7},{7,4},{8,9},{9,10},{10,1... | collective-permute-start | bytes 1179656 | tf_op jit(solution)/shard_map/ppermute | solution.py:38
  196.3 17.5 %collective-permute-start.17 = (bf16[128,1536]{1,0:T(8,128)(2,1)S(1)}, bf16[128,1536]{1,0:T(8,128)(2,1)S(1)}, u32[]{:S(2)}, u32[]{:S(2)}) collective-permute-start(bf16[128,1536]{1,0:T(8,128)(2,1)S(1)} %get-tuple-element.65), channel_id=1, source_target_pairs={{0,2},{1,3},{2,0},{3,1},{4,6},{5,7},{6,4},{7,5},{8,10},{9,11},{10,... | collective-permute-start | bytes 1179656 | tf_op jit(solution)/shard_map/ppermute | solution.py:38
  196.6 17.8 %collective-permute-start.18 = (bf16[128,1536]{1,0:T(8,128)(2,1)S(1)}, bf16[128,1536]{1,0:T(8,128)(2,1)S(1)}, u32[]{:S(2)}, u32[]{:S(2)}) collective-permute-start(bf16[128,1536]{1,0:T(8,128)(2,1)S(1)} %get-tuple-element.64), channel_id=1, source_target_pairs={{0,3},{1,0},{2,1},{3,2},{4,7},{5,4},{6,5},{7,6},{8,11},{9,8},{10,9... | collective-permute-start | bytes 1179656 | tf_op jit(solution)/shard_map/ppermute | solution.py:38
  (43 other events, 916.1 us)
Sparse Core Ops, SparseCore 0:
  9.6 80.4 all-gather.3
  92.2 50.6 all-gather.5
  145.1 39.5 all-gather.7
